TPU v7x, 128 devices: a whole 4x4x4 slice. The times are simulated.
128 devices in a mesh: row: 8 (over z, core), col: 8 (over y_lo, x), dep: 2 (over y_hi).
Axes of the slice: x: 4, y: 4 (y_hi: 2, y_lo: 2; y = y_hi * 2 + y_lo), z: 4, core: 2. Of those that a mesh axis runs over, the one named last changes fastest.
Arguments:
- tokens: bfloat16 [2048, 8192], P(('dep', 'col'), 'row'), may hold values from -6 to 6
- gate_weight: bfloat16 [8192, 14336], P('row', 'col'), may hold values from -0.0625 to 0.0625
- up_weight: bfloat16 [8192, 14336], P('row', 'col'), may hold values from -0.0625 to 0.0625
- cotangent: bfloat16 [2048, 14336], P(('dep', 'row'), 'col'), may hold values from -6 to 6
Outputs:
- hidden: bfloat16 [2048, 14336], P(('dep', 'row'), 'col')
- grad_tokens: bfloat16 [2048, 8192], P(('dep', 'col'), 'row')
- grad_gate_weight: bfloat16 [8192, 14336], P('row', ('col', 'dep'))
- grad_up_weight: bfloat16 [8192, 14336], P('row', ('col', 'dep'))
All inputs are finite; a program needn't handle non-finite values.
Results may differ from a plain program's by a relative error of at most 0.02.
Values may be sent and summed in bfloat16 or wider, within the bound.
No kernel may reach another device: no remote copies, remote signals or barrier semaphores. Data moves between devices by JAX's collectives and lax.ppermute only.
A program may use at most 128 MiB of HBM per device.

v0:
```python
import jax
import jax.numpy as jnp
from jax import lax
from jax.sharding import PartitionSpec as P


def halves(x, dep, half):
    own = lax.dynamic_slice_in_dim(x, dep * half, half, axis=1)
    other = lax.dynamic_slice_in_dim(x, (1 - dep) * half, half, axis=1)
    return (own, other)


def on_device(tokens, gate_weight, up_weight, cotangent):
    width = gate_weight.shape[1]
    half = width // 2
    dep = lax.axis_index("dep")
    n_col = lax.axis_size("col")
    contract = (((0,), (0,)), ((), ()))
    transposed = (((1,), (1,)), ((), ()))
    pair = [(0, 1), (1, 0)]

    def gather_col(block):
        return lax.all_to_all(jnp.tile(block, (n_col, 1)), "col", 0, 0, tiled=True)

    partner_tokens = lax.ppermute(tokens, "dep", pair)
    gathered = gather_col(tokens)
    first = jnp.dot(gathered, gate_weight, preferred_element_type=jnp.float32)
    second = jnp.dot(gathered, up_weight, preferred_element_type=jnp.float32)
    joined = lax.psum_scatter(
        jnp.concatenate([first, second], axis=1).astype(jnp.bfloat16),
        "row",
        scatter_dimension=0,
        tiled=True,
    )
    gathered_partner = gather_col(partner_tokens)
    joined, gathered_partner = lax.optimization_barrier((joined, gathered_partner))
    gate = joined[:, :width]
    up = joined[:, width:]
    upstream = cotangent

    def grads(gate, up, upstream):
        gate, up, upstream = (x.astype(jnp.float32) for x in (gate, up, upstream))
        sigma = jax.nn.sigmoid(gate)
        active = gate * sigma
        grad_gate = (upstream * up * sigma * (1.0 + gate * (1.0 - sigma))).astype(jnp.bfloat16)
        return (grad_gate, (upstream * active).astype(jnp.bfloat16))

    gate_own, gate_other = halves(gate, dep, half)
    up_own, up_other = halves(up, dep, half)
    up_stream_own, up_stream_other = halves(upstream, dep, half)
    grad_gate_other, grad_up_other = grads(gate_other, up_other, up_stream_other)
    payload = jnp.concatenate([grad_gate_other, grad_up_other], axis=1)
    payload, gate_own, up_own, up_stream_own, gate, up = lax.optimization_barrier(
        (payload, gate_own, up_own, up_stream_own, gate, up)
    )
    partner_gate, partner_up = jnp.split(lax.ppermute(payload, "dep", pair), 2, axis=1)
    grad_gate_own, grad_up_own = grads(gate_own, up_own, up_stream_own)
    gate, up = (gate.astype(jnp.float32), up.astype(jnp.float32))
    hidden = (gate * jax.nn.sigmoid(gate) * up).astype(jnp.bfloat16)
    gate_own, up_own, gate_other, up_other = (
        grad_gate_own,
        grad_up_own,
        grad_gate_other,
        grad_up_other,
    )
    full = lax.all_gather(
        jnp.concatenate([gate_own, up_own, gate_other, up_other, partner_gate, partner_up], axis=1),
        "row",
        axis=0,
        tiled=True,
    )
    wg_own, wg_other = halves(gate_weight, dep, half)
    wu_own, wu_other = halves(up_weight, dep, half)
    weights = jnp.concatenate([wg_own, wu_own, wg_other, wu_other], axis=1)
    term = lax.dot_general(
        full[:, : 2 * width], weights, transposed, preferred_element_type=jnp.float32
    )
    term = term.astype(jnp.bfloat16).reshape(n_col, -1, term.shape[1])
    term, gathered, gathered_partner = lax.optimization_barrier((term, gathered, gathered_partner))
    parts = lax.all_to_all(term, "col", 0, 0, tiled=True)
    grad_tokens = parts.astype(jnp.float32).sum(axis=0).astype(jnp.bfloat16)

    def weight_grad(own, partner):
        mine = lax.dot_general(gathered, own, contract, preferred_element_type=jnp.float32)
        theirs = lax.dot_general(
            gathered_partner, partner, contract, preferred_element_type=jnp.float32
        )
        return (
            mine.astype(jnp.bfloat16).astype(jnp.float32)
            + theirs.astype(jnp.bfloat16).astype(jnp.float32)
        ).astype(jnp.bfloat16)

    sum_gate = weight_grad(full[:, :half], full[:, 2 * width : 2 * width + half])
    sum_up = weight_grad(full[:, half:width], full[:, 2 * width + half :])
    return (hidden, grad_tokens, sum_gate, sum_up)


def solution(mesh):
    return jax.shard_map(
        on_device,
        mesh=mesh,
        in_specs=(
            P(("dep", "col"), "row"),
            P("row", "col"),
            P("row", "col"),
            P(("dep", "row"), "col"),
        ),
        out_specs=(
            P(("dep", "row"), "col"),
            P(("dep", "col"), "row"),
            P("row", ("col", "dep")),
            P("row", ("col", "dep")),
        ),
        check_vma=False,
    )
```

profile of v0, /device:TPU:6, one launch (start us, length us, event | category | flops | bytes accessed | tf_op | source)
XLA Modules:
  0.0 237.5 jit_solution(15468545211119573866)
XLA Ops:
  7.2 0.0 reduce-scatter.2.cloned.1.call-start
  7.2 1.2 tile.4
  8.4 0.0 copy-start
  8.4 30.9 %all_to_all.23 = bf16[8,128,1024]{2,1,0:T(8,128)(2,1)S(1)} all-to-all(bf16[8,128,1024]{2,1,0:T(8,128)(2,1)S(1)} %tile.4), channel_id=1, replica_groups=mesh['row'=8,'col'=8,'dep'=2] {'col'}, dimensions={0} | all-to-all | bytes 4194304 | tf_op jit(solution)/shard_map/all_to_all | solution.py:23
  39.4 0.0 copy-start.2
  39.4 0.0 copy-done
  39.4 0.0 copy-start.1
  39.4 4.2 %convolution_convert_fusion = bf16[1024,1792]{1,0:T(8,128)(2,1)S(1)} fusion(bf16[1024,1024]{1,0:T(8,128)(2,1)S(1)} %bitcast.11, bf16[1024,1792]{1,0:T(8,128)(2,1)S(1)} %copy-done), kind=kOutput, calls=%fused_computation.10 | convolution fusion | flops 3759931392 | bytes 9437184 | tf_op jit(solution)/shard_map/dot_general | solution.py:28
  43.5 0.0 copy-done.2
  43.5 0.0 copy-done.1
  43.5 5.4 %convolution_convert_fusion.1 = bf16[1024,1792]{1,0:T(8,128)(2,1)} fusion(bf16[1024,1024]{1,0:T(8,128)(2,1)S(1)} %bitcast.12, bf16[1024,1792]{1,0:T(8,128)(2,1)S(1)} %copy-done.1), kind=kOutput, calls=%fused_computation.11 | convolution fusion | flops 3759931392 | bytes 9437184 | tf_op jit(solution)/shard_map/dot_general | solution.py:27
  48.9 5.5 %pad_maximum_fusion = bf16[1024,3584]{1,0:T(8,128)(2,1)} fusion(bf16[1024,1792]{1,0:T(8,128)(2,1)S(1)} %convolution_convert_fusion, bf16[1024,1792]{1,0:T(8,128)(2,1)} %convolution_convert_fusion.1), kind=kLoop, calls=%fused_computation.2 | loop fusion | flops 14680064 | bytes 14680064 | tf_op jit(solution)/shard_map/concatenate | solution.py:30
  54.5 0.0 copy-start.7
  54.5 0.0 reduce-scatter.2.cloned.1.call-update
  54.5 0.9 copy-done.7
  55.4 2.9 %collective-permute-start = (bf16[128,1024]{1,0:T(8,128)(2,1)S(1)}, bf16[128,1024]{1,0:T(8,128)(2,1)S(1)}, u32[]{:S(2)}, u32[]{:S(2)}) collective-permute-start(bf16[128,1024]{1,0:T(8,128)(2,1)S(1)} %copy-done.7), channel_id=1, source_target_pairs={{0,1},{1,0},{2,3},{3,2},{4,5},{5,4},{6,7},{7,6},{8,9},{9,8},{10,11... | collective-permute-start | bytes 786440 | tf_op jit(solution)/shard_map/ppermute | solution.py:25
  58.3 5.2 %collective-permute-done = bf16[128,1024]{1,0:T(8,128)(2,1)S(1)} collective-permute-done((bf16[128,1024]{1,0:T(8,128)(2,1)S(1)}, bf16[128,1024]{1,0:T(8,128)(2,1)S(1)}, u32[]{:S(2)}, u32[]{:S(2)}) %collective-permute-start) | collective-permute-done | bytes 262176 | tf_op jit(solution)/shard_map/ppermute | solution.py:25
  63.5 1.6 tile.5
  65.1 0.0 copy-start.6
  65.1 5.9 %all-to-all-start.1 = ((bf16[8,128,1024]{2,1,0:T(8,128)(2,1)}), bf16[8,128,1024]{2,1,0:T(8,128)(2,1)S(1)}, u32[]{:S(2)}, u32[]{:S(2)}) async-start(bf16[8,128,1024]{2,1,0:T(8,128)(2,1)} %tile.5), calls=%async_computation.2 | async-start | bytes 4194304 | tf_op jit(solution)/shard_map/all_to_all | solution.py:23
  71.1 0.0 all-gather.2.cloned.1.call-start
  71.1 0.0 copy-done.6
  71.1 22.6 %all-to-all-done.1 = bf16[8,128,1024]{2,1,0:T(8,128)(2,1)S(1)} async-done(((bf16[8,128,1024]{2,1,0:T(8,128)(2,1)}), bf16[8,128,1024]{2,1,0:T(8,128)(2,1)S(1)}, u32[]{:S(2)}, u32[]{:S(2)}) %all-to-all-start.1) | async-done | bytes 2097184 | tf_op jit(solution)/shard_map/all_to_all | solution.py:23
  93.7 0.0 copy-start.4
  93.7 10.4 %reduce-scatter.2.cloned.1.call-done = bf16[128,3584]{1,0:T(8,128)(2,1)} async-done(((bf16[1024,3584]{1,0:T(8,128)(2,1)}), bf16[128,3584]{1,0:T(8,128)(2,1)}) %reduce-scatter.2.cloned.1.call-update) | async-done | bytes 917520 | tf_op jit(solution)/shard_map/reduce_scatter | solution.py:29
  104.1 0.0 copy-done.4
  104.1 1.2 fusion.50
  105.4 0.3 fusion.33
  105.7 3.1 %collective-permute-start.1 = (bf16[128,1792]{1,0:T(8,128)(2,1)S(1)}, bf16[128,1792]{1,0:T(8,128)(2,1)S(1)}, u32[]{:S(2)}, u32[]{:S(2)}) collective-permute-start(bf16[128,1792]{1,0:T(8,128)(2,1)S(1)} %pad_maximum_fusion.1), channel_id=1, source_target_pairs={{0,1},{1,0},{2,3},{3,2},{4,5},{5,4},{6,7},{7,6},{8,9},{9,8},{10,11... | collective-permute-start | bytes 1376264 | tf_op jit(solution)/shard_map/ppermute | solution.py:56
  108.8 0.9 fusion.48
  109.7 0.8 fusion.47
  110.6 0.7 constant_dynamic-update-slice_fusion.2
  111.3 0.7 constant_dynamic-update-slice_fusion.1
  112.0 6.8 %collective-permute-done.1 = bf16[128,1792]{1,0:T(8,128)(2,1)S(1)} collective-permute-done((bf16[128,1792]{1,0:T(8,128)(2,1)S(1)}, bf16[128,1792]{1,0:T(8,128)(2,1)S(1)}, u32[]{:S(2)}, u32[]{:S(2)}) %collective-permute-start.1) | collective-permute-done | bytes 458784 | tf_op jit(solution)/shard_map/ppermute | solution.py:56
  118.9 0.8 constant_dynamic-update-slice_fusion
  119.7 0.0 all-gather.2.cloned.1.call-update
  119.7 5.8 %constant_dynamic-slice_fusion.1 = (bf16[1024,896]{1,0:T(8,128)(2,1)S(1)}, bf16[1024,896]{1,0:T(8,128)(2,1)}, bf16[1024,896]{1,0:T(8,128)(2,1)}, bf16[1024,896]{1,0:T(8,128)(2,1)}) fusion(bf16[1024,1792]{1,0:T(8,128)(2,1)} %param.6, s32[]{:T(128)S(6)} %select_n.5, s32[]{:T(128)S(6)} %select_n.4, bf16[1024,1792]{1,0:T(8,128)(2,1)} %param.5), kind=kLoop, calls=%fused_computation.63 | loop fusion | bytes 14680072 | tf_op jit(solution)/shard_map/dynamic_slice | solution.py:8
  125.5 1.0 fusion.30
  126.6 54.8 %all-gather.2.cloned.1.call-done = bf16[1024,5376]{1,0:T(8,128)(2,1)} async-done(((bf16[128,5376]{1,0:T(8,128)(2,1)}), bf16[1024,5376]{1,0:T(8,128)(2,1)}) %all-gather.2.cloned.1.call-update) | async-done | bytes 11010064 | tf_op jit(solution)/shard_map/all_gather | solution.py:66
  181.3 12.9 %fusion.9 = bf16[1024,1024]{1,0:T(8,128)(2,1)} fusion(bf16[1024,896]{1,0:T(8,128)(2,1)} %get-tuple-element.29, bf16[1024,896]{1,0:T(8,128)(2,1)} %get-tuple-element.36, bf16[1024,896]{1,0:T(8,128)(2,1)S(1)} %get-tuple-element.28, bf16[1024,896]{1,0:T(8,128)(2,1)} %get-tuple-element.37, bf16[1024,5376]{1,0:T(8,128)(2,1)} %all-gather.2.cloned.1.call-done), kind=kOutput, calls=%fused_computation.14 | convolution fusion | flops 7546601472 | bytes 16777216 | tf_op jit(solution)/shard_map/dot_general | solution.py:75
  194.2 5.7 %all-to-all-start.2 = ((bf16[8,128,1024]{2,1,0:T(8,128)(2,1)}), bf16[8,128,1024]{2,1,0:T(8,128)(2,1)S(1)}, u32[]{:S(2)}, u32[]{:S(2)}) async-start(bf16[8,128,1024]{2,1,0:T(8,128)(2,1)} %bitcast.17), calls=%async_computation.3 | async-start | bytes 4194304 | tf_op jit(solution)/shard_map/all_to_all | solution.py:80
  200.0 0.0 copy-start.3
  200.0 4.7 %fusion.16 = bf16[1024,896]{1,0:T(8,128)(2,1)S(1)} fusion(bf16[1024,1024]{1,0:T(8,128)(2,1)} %bitcast.13, bf16[1024,5376]{1,0:T(8,128)(2,1)} %all-gather.2.cloned.1.call-done), kind=kOutput, calls=%fused_computation.17 | convolution fusion | flops 1879048192 | bytes 5767168 | tf_op jit(solution)/shard_map/dot_general | solution.py:84
  204.6 0.0 copy-done.3
  204.7 0.0 copy-start.5
  204.7 4.1 %fusion.20 = bf16[1024,896]{1,0:T(8,128)(2,1)S(1)} fusion(bf16[1024,1024]{1,0:T(8,128)(2,1)S(1)} %bitcast.14, bf16[1024,5376]{1,0:T(8,128)(2,1)} %all-gather.2.cloned.1.call-done), kind=kOutput, calls=%fused_computation.21 | convolution fusion | flops 1879048192 | bytes 5767168 | tf_op jit(solution)/shard_map/dot_general | solution.py:84
  208.7 0.0 copy-done.5
  208.8 5.2 %add_convert_fusion.1 = bf16[1024,896]{1,0:T(8,128)(2,1)} fusion(bf16[1024,896]{1,0:T(8,128)(2,1)S(1)} %fusion.20, bf16[1024,1024]{1,0:T(8,128)(2,1)S(1)} %bitcast.15, bf16[1024,5376]{1,0:T(8,128)(2,1)} %all-gather.2.cloned.1.call-done), kind=kOutput, calls=%fused_computation.13 | convolution fusion | flops 1883635712 | bytes 7602176 | tf_op jit(solution)/shard_map/dot_general | solution.py:85
  214.0 5.2 %add_convert_fusion = bf16[1024,896]{1,0:T(8,128)(2,1)} fusion(bf16[1024,896]{1,0:T(8,128)(2,1)S(1)} %fusion.16, bf16[1024,1024]{1,0:T(8,128)(2,1)S(1)} %bitcast.16, bf16[1024,5376]{1,0:T(8,128)(2,1)} %all-gather.2.cloned.1.call-done), kind=kOutput, calls=%fused_computation.12 | convolution fusion | flops 1883635712 | bytes 7602176 | tf_op jit(solution)/shard_map/dot_general | solution.py:85
  219.2 10.4 %all-to-all-done.2 = bf16[8,128,1024]{2,1,0:T(8,128)(2,1)S(1)} async-done(((bf16[8,128,1024]{2,1,0:T(8,128)(2,1)}), bf16[8,128,1024]{2,1,0:T(8,128)(2,1)S(1)}, u32[]{:S(2)}, u32[]{:S(2)}) %all-to-all-start.2) | async-done | bytes 2097184 | tf_op jit(solution)/shard_map/all_to_all | solution.py:80
  229.6 1.1 reduce_sum.12
  (3 shorter events, 0.1 us)
Async XLA Ops:
  7.2 96.9 %reduce-scatter.2.cloned.1.call-start = ((), (), s32[]{:S(2)}) async-start(), calls=%async_computation.4 | async-start | bytes 8257536 | tf_op jit(solution)/shard_map/reduce_scatter | solution.py:29
  8.4 30.9 %copy-start = (bf16[1024,1792]{1,0:T(8,128)(2,1)S(1)}, bf16[1024,1792]{1,0:T(8,128)(2,1)}, u32[]{:S(2)}) copy-start(bf16[1024,1792]{1,0:T(8,128)(2,1)} %param.6) | copy-start | bytes 11010052
  39.4 4.2 %copy-start.2 = (bf16[8,128,1024]{2,1,0:T(8,128)(2,1)}, bf16[8,128,1024]{2,1,0:T(8,128)(2,1)S(1)}, u32[]{:S(2)}) copy-start(bf16[8,128,1024]{2,1,0:T(8,128)(2,1)S(1)} %all_to_all.23) | copy-start | bytes 6291460
  39.4 4.2 %copy-start.1 = (bf16[1024,1792]{1,0:T(8,128)(2,1)S(1)}, bf16[1024,1792]{1,0:T(8,128)(2,1)}, u32[]{:S(2)}) copy-start(bf16[1024,1792]{1,0:T(8,128)(2,1)} %param.5) | copy-start | bytes 11010052
  54.5 0.9 copy-start.7
  55.4 8.1 %collective-permute-start = (bf16[128,1024]{1,0:T(8,128)(2,1)S(1)}, bf16[128,1024]{1,0:T(8,128)(2,1)S(1)}, u32[]{:S(2)}, u32[]{:S(2)}) collective-permute-start(bf16[128,1024]{1,0:T(8,128)(2,1)S(1)} %copy-done.7), channel_id=1, source_target_pairs={{0,1},{1,0},{2,3},{3,2},{4,5},{5,4},{6,7},{7,6},{8,9},{9,8},{10,11... | collective-permute-start | bytes 786440 | tf_op jit(solution)/shard_map/ppermute | solution.py:25
  65.1 5.9 %copy-start.6 = (bf16[128,1792]{1,0:T(8,128)(2,1)S(1)}, bf16[128,1792]{1,0:T(8,128)(2,1)}, u32[]{:S(2)}) copy-start(bf16[128,1792]{1,0:T(8,128)(2,1)} %param.7) | copy-start | bytes 1376260
  65.1 28.5 %all-to-all-start.1 = ((bf16[8,128,1024]{2,1,0:T(8,128)(2,1)}), bf16[8,128,1024]{2,1,0:T(8,128)(2,1)S(1)}, u32[]{:S(2)}, u32[]{:S(2)}) async-start(bf16[8,128,1024]{2,1,0:T(8,128)(2,1)} %tile.5), calls=%async_computation.2 | async-start | bytes 4194304 | tf_op jit(solution)/shard_map/all_to_all | solution.py:23
  71.1 110.3 %all-gather.2.cloned.1.call-start = ((), (), s32[]{:S(2)}) async-start(), calls=%async_computation.5 | async-start | bytes 12386304 | tf_op jit(solution)/shard_map/all_gather | solution.py:66
  93.7 10.4 %copy-start.4 = (bf16[8,128,1024]{2,1,0:T(8,128)(2,1)}, bf16[8,128,1024]{2,1,0:T(8,128)(2,1)S(1)}, u32[]{:S(2)}) copy-start(bf16[8,128,1024]{2,1,0:T(8,128)(2,1)S(1)} %all-to-all-done.1) | copy-start | bytes 6291460
  105.7 13.2 %collective-permute-start.1 = (bf16[128,1792]{1,0:T(8,128)(2,1)S(1)}, bf16[128,1792]{1,0:T(8,128)(2,1)S(1)}, u32[]{:S(2)}, u32[]{:S(2)}) collective-permute-start(bf16[128,1792]{1,0:T(8,128)(2,1)S(1)} %pad_maximum_fusion.1), channel_id=1, source_target_pairs={{0,1},{1,0},{2,3},{3,2},{4,5},{5,4},{6,7},{7,6},{8,9},{9,8},{10,11... | collective-permute-start | bytes 1376264 | tf_op jit(solution)/shard_map/ppermute | solution.py:56
  194.2 35.3 %all-to-all-start.2 = ((bf16[8,128,1024]{2,1,0:T(8,128)(2,1)}), bf16[8,128,1024]{2,1,0:T(8,128)(2,1)S(1)}, u32[]{:S(2)}, u32[]{:S(2)}) async-start(bf16[8,128,1024]{2,1,0:T(8,128)(2,1)} %bitcast.17), calls=%async_computation.3 | async-start | bytes 4194304 | tf_op jit(solution)/shard_map/all_to_all | solution.py:80
  200.0 4.7 %copy-start.3 = (bf16[8,128,1024]{2,1,0:T(8,128)(2,1)S(1)}, bf16[8,128,1024]{2,1,0:T(8,128)(2,1)}, u32[]{:S(2)}) copy-start(bf16[8,128,1024]{2,1,0:T(8,128)(2,1)} %copy-done.2) | copy-start | bytes 6291460
  204.7 4.1 %copy-start.5 = (bf16[8,128,1024]{2,1,0:T(8,128)(2,1)S(1)}, bf16[8,128,1024]{2,1,0:T(8,128)(2,1)}, u32[]{:S(2)}) copy-start(bf16[8,128,1024]{2,1,0:T(8,128)(2,1)} %copy-done.4) | copy-start | bytes 6291460
Sparse Core Ops, SparseCore 0:
  54.6 49.4 reduce-scatter.1
  119.9 61.4 all-gather.1
where the time goes:
time: 238 us
  waiting for transfers between devices  110 us (46%)
  matrix products  41.6 us (17%)
  blocking collectives  30.9 us (13%)
  starting transfers between devices  17.7 us (7%)
  between operations  14.2 us (6%)
  local copies, waits for them, and re-layouts  13.2 us (6%)
  other arithmetic  9.78 us (4%)
    all_gather x1, waiting for transfers between devices, on_device(): lax.all_gather(jnp.concatenate([gate_own, up_own, gate_other, up_other, p...  54.8 us
    all_to_all x1, blocking collectives, gather_col(): return lax.all_to_all(jnp.tile(block, (n_col, 1)), 'col', 0, 0, tiled=True)  30.9 us
    all_to_all x1, waiting for transfers between devices, gather_col(): return lax.all_to_all(jnp.tile(block, (n_col, 1)), 'col', 0, 0, tiled=True)  22.6 us
    dot_general x1, matrix products, on_device(): lax.dot_general(full[:, :2 * width], weights, transposed, preferred_eleme...  12.9 us
    dot_general x2, matrix products, weight_grad(): lax.dot_general(gathered_partner, partner, contract, preferred_element_ty...  10.4 us
    reduce_scatter x1, waiting for transfers between devices, on_device(): lax.psum_scatter(jnp.concatenate([first, second], axis=1).astype(jnp.bflo...  10.4 us
    all_to_all x1, waiting for transfers between devices, on_device(): parts = lax.all_to_all(term, 'col', 0, 0, tiled=True)  10.4 us
    dot_general x2, matrix products, weight_grad(): lax.dot_general(gathered, own, contract, preferred_element_type=jnp.float32)  8.74 us
  transfers between devices with their start and end apart: 6, of which 6 were waited for; matrix products, arithmetic and copies ran while one was open for 13% of the time, Pallas kernels for 0%

commit v1 on v0

--- a/solution.py
+++ b/solution.py
@@ -63,11 +63,22 @@
         grad_gate_other,
         grad_up_other,
     )
-    full = lax.all_gather(
-        jnp.concatenate([gate_own, up_own, gate_other, up_other, partner_gate, partner_up], axis=1),
-        "row",
-        axis=0,
-        tiled=True,
+    full = jnp.concatenate(
+        lax.all_to_all(
+            jnp.stack(
+                [
+                    jnp.concatenate(
+                        [gate_own, up_own, gate_other, up_other, partner_gate, partner_up], axis=1
+                    )
+                ]
+                * lax.axis_size("row"),
+                0,
+            ),
+            "row",
+            0,
+            0,
+        ),
+        0,
     )
     wg_own, wg_other = halves(gate_weight, dep, half)
     wu_own, wu_other = halves(up_weight, dep, half)

time: 238 us -> 305 us (1.28)
  waiting for transfers between devices: 110 us -> 171 us
  starting transfers between devices: 17.7 us -> 22.8 us
    all_to_all x0 -> x1, waiting for transfers between devices: none -> 116 us  [on_device(): lax.all_to_all(jnp.stack([jnp.concatenate([gate_own, up_own, gate_other,...]
    all_gather x1 -> x0, waiting for transfers between devices: 54.8 us -> none  [on_device(): lax.all_gather(jnp.concatenate([gate_own, up_own, gate_other, up_other, p...]
    all_to_all x0 -> x1, starting transfers between devices: none -> 5.2 us  [on_device(): lax.all_to_all(jnp.stack([jnp.concatenate([gate_own, up_own, gate_other,...]
    another operation x0 -> x1, local copies, waits for them, and re-layouts: none -> 4.74 us  [on_device(): jnp.stack([jnp.concatenate([gate_own, up_own, gate_other, up_other, partn...]
    all_to_all x1, waiting for transfers between devices: 10.4 us -> 6.86 us  [on_device(): parts = lax.all_to_all(term, 'col', 0, 0, tiled=True)]
  transfers between devices with their start and end apart: 6 -> 6, of which waited for: 6 -> 6; matrix products, arithmetic and copies ran while one was open for 13% -> 9% of each run, Pallas kernels for 0% -> 0%
where the time goes in v1:
time: 305 us; the launch traced here: 304 us
  waiting for transfers between devices  171 us (56%)
  matrix products  41.6 us (14%)
  blocking collectives  30.9 us (10%)
  starting transfers between devices  22.8 us (7%)
  local copies, waits for them, and re-layouts  15.7 us (5%)
  between operations  14.2 us (5%)
  other arithmetic  8.38 us (3%)
    all_to_all x1, waiting for transfers between devices, on_device(): lax.all_to_all(jnp.stack([jnp.concatenate([gate_own, up_own, gate_other,...  116 us
    all_to_all x1, blocking collectives, gather_col(): return lax.all_to_all(jnp.tile(block, (n_col, 1)), 'col', 0, 0, tiled=True)  30.9 us
    all_to_all x1, waiting for transfers between devices, gather_col(): return lax.all_to_all(jnp.tile(block, (n_col, 1)), 'col', 0, 0, tiled=True)  22.6 us
    dot_general x1, matrix products, on_device(): lax.dot_general(full[:, :2 * width], weights, transposed, preferred_eleme...  12.9 us
    dot_general x2, matrix products, weight_grad(): lax.dot_general(gathered_partner, partner, contract, preferred_element_ty...  10.4 us
    reduce_scatter x1, waiting for transfers between devices, on_device(): lax.psum_scatter(jnp.concatenate([first, second], axis=1).astype(jnp.bflo...  10.4 us
    ppermute x1, waiting for transfers between devices, on_device(): lax.ppermute(payload, 'dep', pair)  9.62 us
    dot_general x2, matrix products, weight_grad(): lax.dot_general(gathered, own, contract, preferred_element_type=jnp.float32)  8.74 us
  transfers between devices with their start and end apart: 6, of which 6 were waited for; matrix products, arithmetic and copies ran while one was open for 9% of the time, Pallas kernels for 0%

profile of v1, /device:TPU:6, one launch (start us, length us, event | category | flops | bytes accessed | tf_op | source)
XLA Modules:
  0.0 304.1 jit_solution(3370863977094159383)
XLA Ops:
  7.2 0.0 reduce-scatter.2.cloned.1.call-start
  7.2 1.2 tile.4
  8.4 0.0 copy-start
  8.4 30.9 %all_to_all.28 = bf16[8,128,1024]{2,1,0:T(8,128)(2,1)S(1)} all-to-all(bf16[8,128,1024]{2,1,0:T(8,128)(2,1)S(1)} %tile.4), channel_id=1, replica_groups=mesh['row'=8,'col'=8,'dep'=2] {'col'}, dimensions={0} | all-to-all | bytes 4194304 | tf_op jit(solution)/shard_map/all_to_all | solution.py:23
  39.4 0.0 copy-start.2
  39.4 0.0 copy-done
  39.4 0.0 copy-start.1
  39.4 4.2 %convolution_convert_fusion = bf16[1024,1792]{1,0:T(8,128)(2,1)S(1)} fusion(bf16[1024,1024]{1,0:T(8,128)(2,1)S(1)} %bitcast.12, bf16[1024,1792]{1,0:T(8,128)(2,1)S(1)} %copy-done), kind=kOutput, calls=%fused_computation.10 | convolution fusion | flops 3759931392 | bytes 9437184 | tf_op jit(solution)/shard_map/dot_general | solution.py:28
  43.5 0.0 copy-done.2
  43.5 0.0 copy-done.1
  43.5 5.4 %convolution_convert_fusion.1 = bf16[1024,1792]{1,0:T(8,128)(2,1)} fusion(bf16[1024,1024]{1,0:T(8,128)(2,1)S(1)} %bitcast.13, bf16[1024,1792]{1,0:T(8,128)(2,1)S(1)} %copy-done.1), kind=kOutput, calls=%fused_computation.11 | convolution fusion | flops 3759931392 | bytes 9437184 | tf_op jit(solution)/shard_map/dot_general | solution.py:27
  48.9 5.6 %pad_maximum_fusion = bf16[1024,3584]{1,0:T(8,128)(2,1)} fusion(bf16[1024,1792]{1,0:T(8,128)(2,1)S(1)} %convolution_convert_fusion, bf16[1024,1792]{1,0:T(8,128)(2,1)} %convolution_convert_fusion.1), kind=kLoop, calls=%fused_computation.2 | loop fusion | flops 14680064 | bytes 14680064 | tf_op jit(solution)/shard_map/concatenate | solution.py:30
  54.5 0.0 copy-start.7
  54.5 0.0 reduce-scatter.2.cloned.1.call-update
  54.5 0.9 copy-done.7
  55.4 2.9 collective-permute-start
  58.3 5.2 %collective-permute-done = bf16[128,1024]{1,0:T(8,128)(2,1)S(1)} collective-permute-done((bf16[128,1024]{1,0:T(8,128)(2,1)S(1)}, bf16[128,1024]{1,0:T(8,128)(2,1)S(1)}, u32[]{:S(2)}, u32[]{:S(2)}) %collective-permute-start) | collective-permute-done | bytes 262176 | tf_op jit(solution)/shard_map/ppermute | solution.py:25
  63.5 1.7 tile.5
  65.1 0.0 copy-start.6
  65.1 5.9 %all-to-all-start.1 = ((bf16[8,128,1024]{2,1,0:T(8,128)(2,1)}), bf16[8,128,1024]{2,1,0:T(8,128)(2,1)S(1)}, u32[]{:S(2)}, u32[]{:S(2)}) async-start(bf16[8,128,1024]{2,1,0:T(8,128)(2,1)} %tile.5), calls=%async_computation.2 | async-start | bytes 4194304 | tf_op jit(solution)/shard_map/all_to_all | solution.py:23
  71.0 0.0 copy-done.6
  71.1 22.6 %all-to-all-done.1 = bf16[8,128,1024]{2,1,0:T(8,128)(2,1)S(1)} async-done(((bf16[8,128,1024]{2,1,0:T(8,128)(2,1)}), bf16[8,128,1024]{2,1,0:T(8,128)(2,1)S(1)}, u32[]{:S(2)}, u32[]{:S(2)}) %all-to-all-start.1) | async-done | bytes 2097184 | tf_op jit(solution)/shard_map/all_to_all | solution.py:23
  93.7 0.0 copy-start.4
  93.7 10.4 %reduce-scatter.2.cloned.1.call-done = bf16[128,3584]{1,0:T(8,128)(2,1)} async-done(((bf16[1024,3584]{1,0:T(8,128)(2,1)}), bf16[128,3584]{1,0:T(8,128)(2,1)}) %reduce-scatter.2.cloned.1.call-update) | async-done | bytes 917520 | tf_op jit(solution)/shard_map/reduce_scatter | solution.py:29
  104.1 0.0 copy-done.4
  104.1 1.2 fusion.50
  105.4 0.3 fusion.33
  105.7 3.1 %collective-permute-start.1 = (bf16[128,1792]{1,0:T(8,128)(2,1)S(1)}, bf16[128,1792]{1,0:T(8,128)(2,1)S(1)}, u32[]{:S(2)}, u32[]{:S(2)}) collective-permute-start(bf16[128,1792]{1,0:T(8,128)(2,1)S(1)} %pad_maximum_fusion.1), channel_id=1, source_target_pairs={{0,1},{1,0},{2,3},{3,2},{4,5},{5,4},{6,7},{7,6},{8,9},{9,8},{10,11... | collective-permute-start | bytes 1376264 | tf_op jit(solution)/shard_map/ppermute | solution.py:56
  108.8 0.2 fusion.48
  109.0 0.2 fusion.47
  109.2 9.6 %collective-permute-done.1 = bf16[128,1792]{1,0:T(8,128)(2,1)S(1)} collective-permute-done((bf16[128,1792]{1,0:T(8,128)(2,1)S(1)}, bf16[128,1792]{1,0:T(8,128)(2,1)S(1)}, u32[]{:S(2)}, u32[]{:S(2)}) %collective-permute-start.1) | collective-permute-done | bytes 458784 | tf_op jit(solution)/shard_map/ppermute | solution.py:56
  118.9 4.7 %stack.2 = bf16[8,128,5376]{2,1,0:T(8,128)(2,1)} broadcast(bf16[128,5376]{1,0:T(8,128)(2,1)S(1)} %constant_dynamic-update-slice_fusion), dimensions={1,2} | broadcast | bytes 12386304 | tf_op jit(solution)/shard_map/stack | solution.py:68
  123.6 5.2 %all-to-all-start.2 = ((bf16[8,128,5376]{2,1,0:T(8,128)(2,1)}), bf16[8,128,5376]{2,1,0:T(8,128)(2,1)}, u32[]{:S(2)}, u32[]{:S(2)}) async-start(bf16[8,128,5376]{2,1,0:T(8,128)(2,1)} %stack.2), calls=%async_computation.3 | async-start | bytes 22020096 | tf_op jit(solution)/shard_map/all_to_all | solution.py:67
  128.8 5.8 %constant_dynamic-slice_fusion.1 = (bf16[1024,896]{1,0:T(8,128)(2,1)S(1)}, bf16[1024,896]{1,0:T(8,128)(2,1)}, bf16[1024,896]{1,0:T(8,128)(2,1)}, bf16[1024,896]{1,0:T(8,128)(2,1)}) fusion(bf16[1024,1792]{1,0:T(8,128)(2,1)} %param.6, s32[]{:T(128)S(6)} %select_n.5, s32[]{:T(128)S(6)} %select_n.4, bf16[1024,1792]{1,0:T(8,128)(2,1)} %param.5), kind=kLoop, calls=%fused_computation.63 | loop fusion | bytes 14680072 | tf_op jit(solution)/shard_map/dynamic_slice | solution.py:8
  134.6 1.0 fusion.30
  135.6 115.9 %all-to-all-done.2 = bf16[8,128,5376]{2,1,0:T(8,128)(2,1)} async-done(((bf16[8,128,5376]{2,1,0:T(8,128)(2,1)}), bf16[8,128,5376]{2,1,0:T(8,128)(2,1)}, u32[]{:S(2)}, u32[]{:S(2)}) %all-to-all-start.2) | async-done | bytes 11010080 | tf_op jit(solution)/shard_map/all_to_all | solution.py:67
  251.5 12.9 %fusion.9 = bf16[1024,1024]{1,0:T(8,128)(2,1)} fusion(bf16[1024,896]{1,0:T(8,128)(2,1)} %get-tuple-element.29, bf16[1024,896]{1,0:T(8,128)(2,1)} %get-tuple-element.36, bf16[1024,896]{1,0:T(8,128)(2,1)S(1)} %get-tuple-element.28, bf16[1024,896]{1,0:T(8,128)(2,1)} %get-tuple-element.37, bf16[1024,5376]{1,0:T(8,128)(2,1)} %bitcast.2), kind=kOutput, calls=%fused_computation.14 | convolution fusion | flops 7546601472 | bytes 16777216 | tf_op jit(solution)/shard_map/dot_general | solution.py:86
  264.4 5.7 %all-to-all-start.3 = ((bf16[8,128,1024]{2,1,0:T(8,128)(2,1)}), bf16[8,128,1024]{2,1,0:T(8,128)(2,1)S(1)}, u32[]{:S(2)}, u32[]{:S(2)}) async-start(bf16[8,128,1024]{2,1,0:T(8,128)(2,1)} %bitcast.18), calls=%async_computation.4 | async-start | bytes 4194304 | tf_op jit(solution)/shard_map/all_to_all | solution.py:91
  270.1 0.0 copy-start.3
  270.1 4.7 %fusion.16 = bf16[1024,896]{1,0:T(8,128)(2,1)S(1)} fusion(bf16[1024,1024]{1,0:T(8,128)(2,1)} %bitcast.14, bf16[1024,5376]{1,0:T(8,128)(2,1)} %bitcast.2), kind=kOutput, calls=%fused_computation.17 | convolution fusion | flops 1879048192 | bytes 5767168 | tf_op jit(solution)/shard_map/dot_general | solution.py:95
  274.8 0.0 copy-done.3
  274.8 0.0 copy-start.5
  274.8 4.1 %fusion.20 = bf16[1024,896]{1,0:T(8,128)(2,1)S(1)} fusion(bf16[1024,1024]{1,0:T(8,128)(2,1)S(1)} %bitcast.15, bf16[1024,5376]{1,0:T(8,128)(2,1)} %bitcast.2), kind=kOutput, calls=%fused_computation.21 | convolution fusion | flops 1879048192 | bytes 5767168 | tf_op jit(solution)/shard_map/dot_general | solution.py:95
  278.9 0.0 copy-done.5
  278.9 5.2 %add_convert_fusion = bf16[1024,896]{1,0:T(8,128)(2,1)} fusion(bf16[1024,896]{1,0:T(8,128)(2,1)S(1)} %fusion.16, bf16[1024,1024]{1,0:T(8,128)(2,1)S(1)} %bitcast.16, bf16[1024,5376]{1,0:T(8,128)(2,1)} %bitcast.2), kind=kOutput, calls=%fused_computation.12 | convolution fusion | flops 1883635712 | bytes 7602176 | tf_op jit(solution)/shard_map/dot_general | solution.py:96
  284.1 5.2 %add_convert_fusion.1 = bf16[1024,896]{1,0:T(8,128)(2,1)} fusion(bf16[1024,896]{1,0:T(8,128)(2,1)S(1)} %fusion.20, bf16[1024,1024]{1,0:T(8,128)(2,1)S(1)} %bitcast.17, bf16[1024,5376]{1,0:T(8,128)(2,1)} %bitcast.2), kind=kOutput, calls=%fused_computation.13 | convolution fusion | flops 1883635712 | bytes 7602176 | tf_op jit(solution)/shard_map/dot_general | solution.py:96
  289.3 6.9 %all-to-all-done.3 = bf16[8,128,1024]{2,1,0:T(8,128)(2,1)S(1)} async-done(((bf16[8,128,1024]{2,1,0:T(8,128)(2,1)}), bf16[8,128,1024]{2,1,0:T(8,128)(2,1)S(1)}, u32[]{:S(2)}, u32[]{:S(2)}) %all-to-all-start.3) | async-done | bytes 2097184 | tf_op jit(solution)/shard_map/all_to_all | solution.py:91
  296.2 1.1 reduce_sum.12
  (6 shorter events, 0.2 us)
Async XLA Ops:
  7.2 96.9 %reduce-scatter.2.cloned.1.call-start = ((), (), s32[]{:S(2)}) async-start(), calls=%async_computation.5 | async-start | bytes 8257536 | tf_op jit(solution)/shard_map/reduce_scatter | solution.py:29
  8.4 30.9 %copy-start = (bf16[1024,1792]{1,0:T(8,128)(2,1)S(1)}, bf16[1024,1792]{1,0:T(8,128)(2,1)}, u32[]{:S(2)}) copy-start(bf16[1024,1792]{1,0:T(8,128)(2,1)} %param.6) | copy-start | bytes 11010052
  39.4 4.2 %copy-start.2 = (bf16[8,128,1024]{2,1,0:T(8,128)(2,1)}, bf16[8,128,1024]{2,1,0:T(8,128)(2,1)S(1)}, u32[]{:S(2)}) copy-start(bf16[8,128,1024]{2,1,0:T(8,128)(2,1)S(1)} %all_to_all.28) | copy-start | bytes 6291460
  39.4 4.2 %copy-start.1 = (bf16[1024,1792]{1,0:T(8,128)(2,1)S(1)}, bf16[1024,1792]{1,0:T(8,128)(2,1)}, u32[]{:S(2)}) copy-start(bf16[1024,1792]{1,0:T(8,128)(2,1)} %param.5) | copy-start | bytes 11010052
  54.5 0.9 copy-start.7
  55.4 8.1 %collective-permute-start = (bf16[128,1024]{1,0:T(8,128)(2,1)S(1)}, bf16[128,1024]{1,0:T(8,128)(2,1)S(1)}, u32[]{:S(2)}, u32[]{:S(2)}) collective-permute-start(bf16[128,1024]{1,0:T(8,128)(2,1)S(1)} %copy-done.7), channel_id=1, source_target_pairs={{0,1},{1,0},{2,3},{3,2},{4,5},{5,4},{6,7},{7,6},{8,9},{9,8},{10,11... | collective-permute-start | bytes 786440 | tf_op jit(solution)/shard_map/ppermute | solution.py:25
  65.1 5.9 %copy-start.6 = (bf16[128,1792]{1,0:T(8,128)(2,1)S(1)}, bf16[128,1792]{1,0:T(8,128)(2,1)}, u32[]{:S(2)}) copy-start(bf16[128,1792]{1,0:T(8,128)(2,1)} %param.7) | copy-start | bytes 1376260
  65.1 28.5 %all-to-all-start.1 = ((bf16[8,128,1024]{2,1,0:T(8,128)(2,1)}), bf16[8,128,1024]{2,1,0:T(8,128)(2,1)S(1)}, u32[]{:S(2)}, u32[]{:S(2)}) async-start(bf16[8,128,1024]{2,1,0:T(8,128)(2,1)} %tile.5), calls=%async_computation.2 | async-start | bytes 4194304 | tf_op jit(solution)/shard_map/all_to_all | solution.py:23
  93.7 10.4 %copy-start.4 = (bf16[8,128,1024]{2,1,0:T(8,128)(2,1)}, bf16[8,128,1024]{2,1,0:T(8,128)(2,1)S(1)}, u32[]{:S(2)}) copy-start(bf16[8,128,1024]{2,1,0:T(8,128)(2,1)S(1)} %all-to-all-done.1) | copy-start | bytes 6291460
  105.7 13.2 %collective-permute-start.1 = (bf16[128,1792]{1,0:T(8,128)(2,1)S(1)}, bf16[128,1792]{1,0:T(8,128)(2,1)S(1)}, u32[]{:S(2)}, u32[]{:S(2)}) collective-permute-start(bf16[128,1792]{1,0:T(8,128)(2,1)S(1)} %pad_maximum_fusion.1), channel_id=1, source_target_pairs={{0,1},{1,0},{2,3},{3,2},{4,5},{5,4},{6,7},{7,6},{8,9},{9,8},{10,11... | collective-permute-start | bytes 1376264 | tf_op jit(solution)/shard_map/ppermute | solution.py:56
  123.6 127.9 %all-to-all-start.2 = ((bf16[8,128,5376]{2,1,0:T(8,128)(2,1)}), bf16[8,128,5376]{2,1,0:T(8,128)(2,1)}, u32[]{:S(2)}, u32[]{:S(2)}) async-start(bf16[8,128,5376]{2,1,0:T(8,128)(2,1)} %stack.2), calls=%async_computation.3 | async-start | bytes 22020096 | tf_op jit(solution)/shard_map/all_to_all | solution.py:67
  264.4 31.8 %all-to-all-start.3 = ((bf16[8,128,1024]{2,1,0:T(8,128)(2,1)}), bf16[8,128,1024]{2,1,0:T(8,128)(2,1)S(1)}, u32[]{:S(2)}, u32[]{:S(2)}) async-start(bf16[8,128,1024]{2,1,0:T(8,128)(2,1)} %bitcast.18), calls=%async_computation.4 | async-start | bytes 4194304 | tf_op jit(solution)/shard_map/all_to_all | solution.py:91
  270.1 4.7 %copy-start.3 = (bf16[8,128,1024]{2,1,0:T(8,128)(2,1)S(1)}, bf16[8,128,1024]{2,1,0:T(8,128)(2,1)}, u32[]{:S(2)}) copy-start(bf16[8,128,1024]{2,1,0:T(8,128)(2,1)} %copy-done.2) | copy-start | bytes 6291460
  274.8 4.1 %copy-start.5 = (bf16[8,128,1024]{2,1,0:T(8,128)(2,1)S(1)}, bf16[8,128,1024]{2,1,0:T(8,128)(2,1)}, u32[]{:S(2)}) copy-start(bf16[8,128,1024]{2,1,0:T(8,128)(2,1)} %copy-done.4) | copy-start | bytes 6291460
Sparse Core Ops, SparseCore 0:
  54.6 49.4 reduce-scatter.1
